TPU v7x, 256 devices: a whole 4x4x8 slice. The times are simulated.
256 devices in a mesh: seq: 64 (over y, z, core), ch: 4 (over x).
Axes of the slice: x: 4, y: 4, z: 8, core: 2. Of those that a mesh axis runs over, the one named last changes fastest.
Arguments:
- query_stream: bfloat16 [16384, 4096], P('seq', 'ch'), may hold values from -16 to 16
- key_stream: bfloat16 [16384, 4096], P('seq', 'ch'), may hold values from -6 to 6
- value_stream: bfloat16 [16384, 4096], P('seq', 'ch'), may hold values from -6 to 6
- filter_taps: float32 [4096, 128], P('ch'), may hold values from -0.5 to 0.5
- out_weight: bfloat16 [4096, 4096], P('seq', 'ch'), may hold values from -0.09375 to 0.09375
- upstream: bfloat16 [16384, 4096], P('seq', 'ch'), may hold values from -6 to 6
Outputs:
- mixed: bfloat16 [16384, 4096], P('seq', 'ch')
- grad_query: bfloat16 [16384, 4096], P('seq', 'ch')
- grad_key: bfloat16 [16384, 4096], P('seq', 'ch')
- grad_value: bfloat16 [16384, 4096], P('seq', 'ch')
- grad_filter: float32 [4096, 128], P('ch')
- grad_weight: float32 [4096, 4096], P('seq', 'ch')
All inputs are finite; a program needn't handle non-finite values.
Results may differ from a plain program's by a relative error of at most 0.0057.
Values may be sent and summed in bfloat16 or wider, within the bound.
No kernel may reach another device: no remote copies, remote signals or barrier semaphores. Data moves between devices by JAX's collectives and lax.ppermute only.
A program may use at most 128 MiB of HBM per device.

v0:
```python
import jax
import jax.numpy as jnp
from jax import lax
from jax.sharding import Mesh
from jax.sharding import PartitionSpec as P

SUB = ("sy", "sz", "sc")


def seq_factors(mesh):
    count = mesh.shape["seq"]
    try:
        devices = list(mesh.devices[:, 0])
        cores = len({d.core_on_chip for d in devices})
        zs = len({d.coords[2] for d in devices})
        if cores * zs and count % (cores * zs) == 0:
            return (count // (cores * zs), zs, cores)
    except Exception:
        pass
    return (count // 16, 8, 2) if count % 16 == 0 else (1, 1, count)


def from_behind(value, axis, count, steps):
    initial, last = (max(0, -steps), min(count, count - steps))
    return lax.ppermute(value, axis, [(source, source + steps) for source in range(initial, last)])


def depthwise(signal, kernel):
    output = lax.conv_general_dilated(
        signal[None],
        kernel[:, None, :],
        (1,),
        "VALID",
        dimension_numbers=("NWC", "WIO", "NWC"),
        feature_group_count=signal.shape[1],
        precision=lax.Precision.HIGHEST,
    )
    return output[0]


def gather_ch(part, count):
    here = lax.axis_index("ch")
    pieces = [part] + [
        lax.ppermute(part, "ch", [(i, (i + k) % count) for i in range(count)])
        for k in range(1, count)
    ]
    stacked = jnp.stack(pieces)[(here - jnp.arange(count)) % count]
    return jnp.concatenate([stacked[j] for j in range(count)], axis=1)


def scatter_ch(whole, count):
    here = lax.axis_index("ch")
    width = whole.shape[1] // count
    total = lax.dynamic_slice_in_dim(whole, here * width, width, 1)
    for k in range(1, count):
        block = lax.dynamic_slice_in_dim(whole, (here + k) % count * width, width, 1)
        total = total + lax.ppermute(block, "ch", [(i, (i + k) % count) for i in range(count)])
    return total


def butterfly_sum(value, factors):
    for axis, size in zip(SUB, factors):
        bit = 1
        while bit < size:
            value = value + lax.ppermute(value, axis, [(i, i ^ bit) for i in range(size)])
            bit *= 2
    return value


def make_body(factors, chs):
    n_seq = factors[0] * factors[1] * factors[2]

    def body(query_stream, key_stream, value_stream, filter_taps, out_weight, upstream):
        rows_here = query_stream.shape[0]
        tap_count = filter_taps.shape[1]
        keyed = (key_stream.astype(jnp.float32) * value_stream.astype(jnp.float32)).astype(
            jnp.bfloat16
        )
        rim_before = from_behind(keyed[rows_here - (tap_count - 1) :], SUB, n_seq, 1)
        front_pad = jnp.concatenate([rim_before, keyed], axis=0).astype(jnp.float32)
        response = depthwise(front_pad, filter_taps.T[::-1])
        query_wide = query_stream.astype(jnp.float32)
        gated = (query_wide * response).astype(jnp.bfloat16)
        gated_full = gather_ch(gated, chs)
        weight_cols = lax.all_gather(out_weight, SUB, axis=0, tiled=True)
        mixed = jnp.dot(gated_full, weight_cols, preferred_element_type=jnp.float32).astype(
            jnp.bfloat16
        )
        partial_terms = lax.dot_general(
            upstream, weight_cols, (((1,), (1,)), ((), ())), preferred_element_type=jnp.float32
        )
        grad_gated = scatter_ch(partial_terms, chs)
        grad_query = (grad_gated * response).astype(jnp.bfloat16)
        grad_response = grad_gated * query_wide
        rim_after = from_behind(grad_response[: tap_count - 1], SUB, n_seq, -1)
        back_pad = jnp.concatenate([grad_response, rim_after], axis=0)
        grad_keyed = depthwise(back_pad, filter_taps.T)
        grad_key = (grad_keyed * value_stream.astype(jnp.float32)).astype(jnp.bfloat16)
        grad_value = (grad_keyed * key_stream.astype(jnp.float32)).astype(jnp.bfloat16)
        filter_local = depthwise(front_pad, grad_response)[::-1].T
        grad_filter = butterfly_sum(filter_local, factors)
        block = out_weight.shape[0]
        columns = lax.slice_in_dim(gated_full, 0, n_seq * block, axis=1)
        columns = columns.reshape((rows_here,) + factors + (block,)).transpose(0, 3, 2, 1, 4)
        columns = columns.reshape(rows_here, n_seq * block)
        partial = lax.dot_general(
            columns, upstream, (((0,), (0,)), ((), ())), preferred_element_type=jnp.float32
        )
        for axis in ("sc", "sz", "sy"):
            partial = lax.psum_scatter(partial, axis, scatter_dimension=0, tiled=True)
        return (mixed, grad_query, grad_key, grad_value, grad_filter, partial)

    return body


def solution(mesh):
    factors = seq_factors(mesh)
    chs = mesh.shape["ch"]
    fine = Mesh(mesh.devices.reshape(factors + (chs,)), SUB + ("ch",))
    rows = P(SUB, "ch")
    in_specs = (rows, rows, rows, P("ch", None), rows, rows)
    out_specs = (rows, rows, rows, rows, P("ch", None), rows)
    return jax.shard_map(
        make_body(factors, chs), mesh=fine, in_specs=in_specs, out_specs=out_specs, check_vma=False
    )
```

profile of v0, /device:TPU:1, one launch (start us, length us, event | category | flops | bytes accessed | tf_op | source)
XLA Modules:
  0.0 451.6 jit_solution(6935114478768854161)
XLA Ops:
  7.2 0.7 all-gather.2.cloned.1.call-update
  8.0 90.0 %all-gather.2.cloned.1.call-done = bf16[4096,1024]{1,0:T(8,128)(2,1)} async-done(((bf16[64,1024]{1,0:T(8,128)(2,1)}), bf16[4096,1024]{1,0:T(8,128)(2,1)}) %all-gather.2.cloned.1.call-update) | async-done | bytes 8388624 | tf_op jit(solution)/shard_map/all_gather | solution.py:85
  98.0 5.7 %fusion.27 = f32[256,4096]{1,0:T(8,128)S(1)} fusion(bf16[256,1024]{1,0:T(8,128)(2,1)S(1)} %copy-done, bf16[4096,1024]{1,0:T(8,128)(2,1)} %all-gather.2.cloned.1.call-done), kind=kOutput, calls=%fused_computation.51 | convolution fusion | flops 2147483648 | bytes 13107200 | tf_op jit(solution)/shard_map/dot_general | solution.py:89
  103.8 1.7 constant_dynamic-slice_fusion.2
  105.5 1.2 copy-done.4
  106.7 1.2 collective-permute-start.4
  107.9 1.5 collective-permute-start.6
  109.4 1.5 collective-permute-start.5
  110.9 21.7 %collective-permute-done.4 = f32[256,1024]{1,0:T(8,128)S(1)} collective-permute-done((f32[256,1024]{1,0:T(8,128)}, f32[256,1024]{1,0:T(8,128)S(1)}, u32[]{:S(2)}, u32[]{:S(2)}) %collective-permute-start.4) | collective-permute-done | bytes 1048608 | tf_op jit(solution)/shard_map/ppermute | solution.py:57
  132.6 1.0 copy-done.10
  133.5 22.5 %collective-permute-done.5 = f32[256,1024]{1,0:T(8,128)} collective-permute-done((f32[256,1024]{1,0:T(8,128)}, f32[256,1024]{1,0:T(8,128)}, u32[]{:S(2)}, u32[]{:S(2)}) %collective-permute-start.5) | collective-permute-done | bytes 1048608 | tf_op jit(solution)/shard_map/ppermute | solution.py:57
  156.1 3.7 convert_multiply_fusion.3
  159.8 3.0 collective-permute-start.7
  163.3 7.3 %collective-permute-done.7 = f32[127,1024]{1,0:T(8,128)} collective-permute-done((f32[127,1024]{1,0:T(8,128)S(1)}, f32[127,1024]{1,0:T(8,128)}, u32[]{:S(2)}, u32[]{:S(2)}) %collective-permute-start.7) | collective-permute-done | bytes 520224 | tf_op jit(solution)/shard_map/ppermute | solution.py:25
  170.6 1.2 maximum_bitcast_fusion.1
  171.9 10.6 %fusion.8 = f32[1,256,1024]{2,0,1:T(1,128)S(1)} fusion(f32[128,1,1024]{2,1,0:T(1,128)S(1)} %copy.20, f32[1,383,1024]{2,1,0:T(8,128)S(1)} %maximum_bitcast_fusion.1), kind=kOutput, calls=%fused_computation.12 | convolution fusion | flops 402653184 | bytes 3141632 | tf_op jit(solution)/shard_map/conv_general_dilated | solution.py:29
  182.5 1.5 fusion.18
  184.0 1.9 collective-permute-start
  186.0 0.7 rev.6
  187.1 2.1 collective-permute-done
  189.4 10.6 %fusion.15 = f32[1,256,1024]{2,0,1:T(1,128)S(1)} fusion(f32[128,1,1024]{2,1,0:T(1,128)S(1)} %copy.18, bf16[1,383,1024]{2,1,0:T(8,128)(2,1)S(1)} %maximum_bitcast_fusion.2), kind=kOutput, calls=%fused_computation.22 | convolution fusion | flops 402653184 | bytes 2357248 | tf_op jit(solution)/shard_map/conv_general_dilated | solution.py:29
  200.1 1.2 fusion.21
  201.3 1.8 collective-permute-start.3
  203.1 0.9 collective-permute-start.2
  204.0 20.9 %collective-permute-done.3 = bf16[256,1024]{1,0:T(8,128)(2,1)S(1)} collective-permute-done((bf16[256,1024]{1,0:T(8,128)(2,1)S(1)}, bf16[256,1024]{1,0:T(8,128)(2,1)S(1)}, u32[]{:S(2)}, u32[]{:S(2)}) %collective-permute-start.3) | collective-permute-done | bytes 524320 | tf_op jit(solution)/shard_map/ppermute | solution.py:44
  224.9 3.9 collective-permute-done.1
  228.8 1.6 pad_maximum_fusion
  230.4 2.3 gather_fusion
  232.7 2.0 fusion.26
  234.7 1.3 copy.23
  236.0 1.2 copy.25
  238.2 8.1 %fusion.28 = f32[4096,1024]{1,0:T(8,128)} fusion(bf16[256,4096]{0,1:T(8,128)(2,1)S(1)} %bitcast.50, bf16[256,1024]{1,0:T(8,128)(2,1)S(1)} %copy-done), kind=kOutput, calls=%fused_computation.52 | convolution fusion | flops 2147483648 | bytes 19398656 | tf_op jit(solution)/shard_map/dot_general | solution.py:106
  246.4 27.5 %reduce-scatter.4.cloned.1.call-done = f32[2048,1024]{1,0:T(8,128)} async-done(((f32[4096,1024]{1,0:T(8,128)}), f32[2048,1024]{1,0:T(8,128)}) %reduce-scatter.4.cloned.1.call-update) | async-done | bytes 8388624 | tf_op jit(solution)/shard_map/reduce_scatter | solution.py:110
  274.0 1.2 copy-done.2
  275.4 10.6 %fusion.13 = f32[1,128,1024]{2,0,1:T(1,128)S(1)} fusion(bf16[1,383,1024]{2,1,0:T(8,128)(2,1)S(1)} %copy-done.12, f32[256,1,1024]{2,0,1:T(8,128)S(1)} %bitcast.51), kind=kOutput, calls=%fused_computation.20 | convolution fusion | flops 402653184 | bytes 2357248 | tf_op jit(solution)/shard_map/conv_general_dilated | solution.py:29
  286.4 1.1 collective-permute-start.8
  287.4 12.3 %collective-permute-done.8 = f32[1024,128]{0,1:T(8,128)S(1)} collective-permute-done((f32[1024,128]{0,1:T(8,128)S(1)}, f32[1024,128]{0,1:T(8,128)S(1)}, u32[]{:S(2)}, u32[]{:S(2)}) %collective-permute-start.8) | collective-permute-done | bytes 524320 | tf_op jit(solution)/shard_map/ppermute | solution.py:65
  299.8 2.5 collective-permute-start.9
  302.3 11.4 %collective-permute-done.9 = f32[1024,128]{0,1:T(8,128)S(1)} collective-permute-done((f32[1024,128]{0,1:T(8,128)S(1)}, f32[1024,128]{0,1:T(8,128)S(1)}, u32[]{:S(2)}, u32[]{:S(2)}) %collective-permute-start.9) | collective-permute-done | bytes 524320 | tf_op jit(solution)/shard_map/ppermute | solution.py:65
  313.8 1.1 collective-permute-start.10
  314.9 66.7 %reduce-scatter.6.cloned.1.call-done = f32[256,1024]{1,0:T(8,128)} async-done(((f32[2048,1024]{1,0:T(8,128)}), f32[256,1024]{1,0:T(8,128)}) %reduce-scatter.6.cloned.1.call-update) | async-done | bytes 1048592 | tf_op jit(solution)/shard_map/reduce_scatter | solution.py:110
  381.7 2.4 collective-permute-start.11
  384.1 23.5 %collective-permute-done.11 = f32[1024,128]{0,1:T(8,128)S(1)} collective-permute-done((f32[1024,128]{0,1:T(8,128)S(1)}, f32[1024,128]{0,1:T(8,128)S(1)}, u32[]{:S(2)}, u32[]{:S(2)}) %collective-permute-start.11) | collective-permute-done | bytes 524320 | tf_op jit(solution)/shard_map/ppermute | solution.py:65
  407.7 4.0 collective-permute-start.12
  411.7 24.2 %collective-permute-done.12 = f32[1024,128]{0,1:T(8,128)S(1)} collective-permute-done((f32[1024,128]{0,1:T(8,128)S(1)}, f32[1024,128]{0,1:T(8,128)S(1)}, u32[]{:S(2)}, u32[]{:S(2)}) %collective-permute-start.12) | collective-permute-done | bytes 524320 | tf_op jit(solution)/shard_map/ppermute | solution.py:65
  436.0 1.5 collective-permute-start.13
  437.4 6.6 %fusion.10 = bf16[256,1024]{1,0:T(8,128)(2,1)} fusion(bf16[4096,1024]{1,0:T(8,128)(2,1)} %all-gather.2.cloned.1.call-done, bf16[256,1024]{1,0:T(8,128)(2,1)S(1)} %copy-done.18, bf16[256,1024]{1,0:T(8,128)(2,1)S(1)} %copy-done.17, bf16[256,1024]{1,0:T(8,128)(2,1)S(1)} %copy-done.16, bf16[256,1024]{1,0:T(8,128)(2,1)S(1)} %copy-done.15), kind=kOutput, calls=%fused_computation.19 | convolution fusion | flops 2156134400 | bytes 11010048 | tf_op jit(solution)/shard_map/dot_general | solution.py:86
  444.1 1.0 copy.28
  (67 shorter events, 3.2 us)
Async XLA Ops:
  7.2 90.8 %copy-start = (bf16[256,1024]{1,0:T(8,128)(2,1)S(1)}, bf16[256,1024]{1,0:T(8,128)(2,1)}, u32[]{:S(2)}) copy-start(bf16[256,1024]{1,0:T(8,128)(2,1)} %param.11) | copy-start | bytes 1572868
  7.2 90.8 %all-gather.2.cloned.1.call-start = ((), (), s32[]{:S(2)}) async-start(), calls=%async_computation.3 | async-start | bytes 8519680 | tf_op jit(solution)/shard_map/all_gather | solution.py:85
  7.9 266.0 %reduce-scatter.4.cloned.1.call-start = ((), (), s32[]{:S(2)}) async-start(), calls=%async_computation.4 | async-start | bytes 25165824 | tf_op jit(solution)/shard_map/reduce_scatter | solution.py:110
  103.8 2.9 copy-start.4
  103.8 52.3 %copy-start.8 = (bf16[256,1024]{1,0:T(8,128)(2,1)S(1)}, bf16[256,1024]{1,0:T(8,128)(2,1)}, u32[]{:S(2)}) copy-start(bf16[256,1024]{1,0:T(8,128)(2,1)} %param.6) | copy-start | bytes 1572868
  106.7 25.9 %collective-permute-start.4 = (f32[256,1024]{1,0:T(8,128)}, f32[256,1024]{1,0:T(8,128)S(1)}, u32[]{:S(2)}, u32[]{:S(2)}) collective-permute-start(f32[256,1024]{1,0:T(8,128)} %get-tuple-element.20), channel_id=1, source_target_pairs={{0,1},{1,2},{2,3},{3,0},{4,5},{5,6},{6,7},{7,4},{8,9},{9,10},{10,1... | collective-permute-start | bytes 3145736 | tf_op jit(solution)/shard_map/ppermute | solution.py:57
  107.9 24.7 %collective-permute-start.6 = (f32[256,1024]{1,0:T(8,128)}, f32[256,1024]{1,0:T(8,128)}, u32[]{:S(2)}, u32[]{:S(2)}) collective-permute-start(f32[256,1024]{1,0:T(8,128)} %get-tuple-element.21), channel_id=1, source_target_pairs={{0,3},{1,0},{2,1},{3,2},{4,7},{5,4},{6,5},{7,6},{8,11},{9,8},{10,9... | collective-permute-start | bytes 3145736 | tf_op jit(solution)/shard_map/ppermute | solution.py:57
  109.4 46.7 %collective-permute-start.5 = (f32[256,1024]{1,0:T(8,128)}, f32[256,1024]{1,0:T(8,128)}, u32[]{:S(2)}, u32[]{:S(2)}) collective-permute-start(f32[256,1024]{1,0:T(8,128)} %get-tuple-element.22), channel_id=1, source_target_pairs={{0,2},{1,3},{2,0},{3,1},{4,6},{5,7},{6,4},{7,5},{8,10},{9,11},{10,... | collective-permute-start | bytes 3145736 | tf_op jit(solution)/shard_map/ppermute | solution.py:57
  110.8 52.0 %copy-start.6 = (f32[1024,128]{1,0:T(8,128)S(1)}, f32[1024,128]{1,0:T(8,128)}, u32[]{:S(2)}) copy-start(f32[1024,128]{1,0:T(8,128)} %param.9) | copy-start | bytes 1572868
  132.6 1.0 copy-start.10
  159.8 12.0 %copy-start.1 = (f32[256,1024]{1,0:T(8,128)}, f32[256,1024]{1,0:T(8,128)S(1)}, u32[]{:S(2)}) copy-start(f32[256,1024]{1,0:T(8,128)S(1)} %get-tuple-element.18) | copy-start | bytes 3145732
  159.8 10.8 %collective-permute-start.7 = (f32[127,1024]{1,0:T(8,128)S(1)}, f32[127,1024]{1,0:T(8,128)}, u32[]{:S(2)}, u32[]{:S(2)}) collective-permute-start(f32[127,1024]{1,0:T(8,128)S(1)} %slice.31), channel_id=1, source_target_pairs={{4,0},{8,4},{12,8},{16,12},{20,16},{24,20},{28,24},{32,28},{36,32}... | collective-permute-start | bytes 1560584 | tf_op jit(solution)/shard_map/ppermute | solution.py:25
  171.8 10.6 %copy-start.13 = (bf16[256,1024]{1,0:T(8,128)(2,1)S(1)}, bf16[256,1024]{1,0:T(8,128)(2,1)}, u32[]{:S(2)}) copy-start(bf16[256,1024]{1,0:T(8,128)(2,1)} %param.7) | copy-start | bytes 1572868
  171.9 10.6 %copy-start.14 = (bf16[256,1024]{1,0:T(8,128)(2,1)S(1)}, bf16[256,1024]{1,0:T(8,128)(2,1)}, u32[]{:S(2)}) copy-start(bf16[256,1024]{1,0:T(8,128)(2,1)} %param.8) | copy-start | bytes 1572868
  182.5 3.5 copy-start.7
  184.0 5.2 %collective-permute-start = (bf16[127,1024]{1,0:T(8,128)(2,1)S(1)}, bf16[127,1024]{1,0:T(8,128)(2,1)S(1)}, u32[]{:S(2)}, u32[]{:S(2)}) collective-permute-start(bf16[127,1024]{1,0:T(8,128)(2,1)S(1)} %slice.26), channel_id=1, source_target_pairs={{0,4},{4,8},{8,12},{12,16},{16,20},{20,24},{24,28},{28,32},{32,36}... | collective-permute-start | bytes 780296 | tf_op jit(solution)/shard_map/ppermute | solution.py:25
  189.4 10.7 %copy-start.11 = (bf16[1,383,1024]{2,1,0:T(8,128)(2,1)}, bf16[1,383,1024]{2,1,0:T(8,128)(2,1)S(1)}, u32[]{:S(2)}) copy-start(bf16[1,383,1024]{2,1,0:T(8,128)(2,1)S(1)} %maximum_bitcast_fusion.2) | copy-start | bytes 2353156
  189.4 10.7 %copy-start.3 = (f32[256,1024]{1,0:T(8,128)S(1)}, f32[256,1024]{1,0:T(8,128)}, u32[]{:S(2)}) copy-start(f32[256,1024]{1,0:T(8,128)} %get-tuple-element.19) | copy-start | bytes 3145732
  189.4 10.7 %copy-start.9 = (bf16[256,1024]{1,0:T(8,128)(2,1)S(1)}, bf16[256,1024]{1,0:T(8,128)(2,1)}, u32[]{:S(2)}) copy-start(bf16[256,1024]{1,0:T(8,128)(2,1)} %param.6) | copy-start | bytes 1572868
  201.3 23.6 %collective-permute-start.3 = (bf16[256,1024]{1,0:T(8,128)(2,1)S(1)}, bf16[256,1024]{1,0:T(8,128)(2,1)S(1)}, u32[]{:S(2)}, u32[]{:S(2)}) collective-permute-start(bf16[256,1024]{1,0:T(8,128)(2,1)S(1)} %get-tuple-element.35), channel_id=1, source_target_pairs={{0,3},{1,0},{2,1},{3,2},{4,7},{5,4},{6,5},{7,6},{8,11},{9,8},{10,9... | collective-permute-start | bytes 1572872 | tf_op jit(solution)/shard_map/ppermute | solution.py:44
  203.1 21.8 %collective-permute-start.2 = (bf16[256,1024]{1,0:T(8,128)(2,1)S(1)}, bf16[256,1024]{1,0:T(8,128)(2,1)S(1)}, u32[]{:S(2)}, u32[]{:S(2)}) collective-permute-start(bf16[256,1024]{1,0:T(8,128)(2,1)S(1)} %get-tuple-element.35), channel_id=1, source_target_pairs={{0,2},{1,3},{2,0},{3,1},{4,6},{5,7},{6,4},{7,5},{8,10},{9,11},{10,... | collective-permute-start | bytes 1572872 | tf_op jit(solution)/shard_map/ppermute | solution.py:44
  204.0 24.9 %collective-permute-start.1 = (bf16[256,1024]{1,0:T(8,128)(2,1)S(1)}, bf16[256,1024]{1,0:T(8,128)(2,1)S(1)}, u32[]{:S(2)}, u32[]{:S(2)}) collective-permute-start(bf16[256,1024]{1,0:T(8,128)(2,1)S(1)} %get-tuple-element.35), channel_id=1, source_target_pairs={{0,1},{1,2},{2,3},{3,0},{4,5},{5,6},{6,7},{7,4},{8,9},{9,10},{10,1... | collective-permute-start | bytes 1572872 | tf_op jit(solution)/shard_map/ppermute | solution.py:44
  234.7 2.6 copy-start.5
  246.4 135.2 %reduce-scatter.6.cloned.1.call-start = ((), (), s32[]{:S(2)}) async-start(), calls=%async_computation.5 | async-start | bytes 9437184 | tf_op jit(solution)/shard_map/reduce_scatter | solution.py:110
  273.9 1.2 copy-start.2
  273.9 1.4 copy-start.12
  274.0 171.1 %reduce-scatter.8.cloned.1.call-start = ((), (), s32[]{:S(2)}) async-start(), calls=%async_computation.6 | async-start | bytes 1310720 | tf_op jit(solution)/shard_map/reduce_scatter | solution.py:110
  286.4 13.3 %collective-permute-start.8 = (f32[1024,128]{0,1:T(8,128)S(1)}, f32[1024,128]{0,1:T(8,128)S(1)}, u32[]{:S(2)}, u32[]{:S(2)}) collective-permute-start(f32[1024,128]{0,1:T(8,128)S(1)} %bitcast.52), channel_id=1, source_target_pairs={{0,64},{64,0},{128,192},{192,128},{1,65},{65,1},{129,193},{193,129... | collective-permute-start | bytes 1572872 | tf_op jit(solution)/shard_map/ppermute | solution.py:65
  299.8 14.0 %collective-permute-start.9 = (f32[1024,128]{0,1:T(8,128)S(1)}, f32[1024,128]{0,1:T(8,128)S(1)}, u32[]{:S(2)}, u32[]{:S(2)}) collective-permute-start(f32[1024,128]{0,1:T(8,128)S(1)} %bitcast_add_fusion), channel_id=1, source_target_pairs={{0,128},{64,192},{128,0},{192,64},{1,129},{65,193},{129,1},{193,65... | collective-permute-start | bytes 1572872 | tf_op jit(solution)/shard_map/ppermute | solution.py:65
  313.8 67.8 %collective-permute-start.10 = (f32[1024,128]{0,1:T(8,128)S(1)}, f32[1024,128]{0,1:T(8,128)S(1)}, u32[]{:S(2)}, u32[]{:S(2)}) collective-permute-start(f32[1024,128]{0,1:T(8,128)S(1)} %add.103), channel_id=1, source_target_pairs={{0,8},{8,0},{16,24},{24,16},{32,40},{40,32},{48,56},{56,48},{1,9},... | collective-permute-start | bytes 1572872 | tf_op jit(solution)/shard_map/ppermute | solution.py:65
  381.6 55.8 %copy-start.15 = (bf16[256,1024]{1,0:T(8,128)(2,1)S(1)}, bf16[256,1024]{1,0:T(8,128)(2,1)}, u32[]{:S(2)}) copy-start(bf16[256,1024]{1,0:T(8,128)(2,1)} %get-tuple-element.24) | copy-start | bytes 1572868
  381.6 55.8 %copy-start.16 = (bf16[256,1024]{1,0:T(8,128)(2,1)S(1)}, bf16[256,1024]{1,0:T(8,128)(2,1)}, u32[]{:S(2)}) copy-start(bf16[256,1024]{1,0:T(8,128)(2,1)} %get-tuple-element.25) | copy-start | bytes 1572868
  381.6 55.8 %copy-start.17 = (bf16[256,1024]{1,0:T(8,128)(2,1)S(1)}, bf16[256,1024]{1,0:T(8,128)(2,1)}, u32[]{:S(2)}) copy-start(bf16[256,1024]{1,0:T(8,128)(2,1)} %get-tuple-element.26) | copy-start | bytes 1572868
  381.6 55.8 %copy-start.18 = (bf16[256,1024]{1,0:T(8,128)(2,1)S(1)}, bf16[256,1024]{1,0:T(8,128)(2,1)}, u32[]{:S(2)}) copy-start(bf16[256,1024]{1,0:T(8,128)(2,1)} %get-tuple-element.27) | copy-start | bytes 1572868
  381.7 25.9 %collective-permute-start.11 = (f32[1024,128]{0,1:T(8,128)S(1)}, f32[1024,128]{0,1:T(8,128)S(1)}, u32[]{:S(2)}, u32[]{:S(2)}) collective-permute-start(f32[1024,128]{0,1:T(8,128)S(1)} %add.104), channel_id=1, source_target_pairs={{0,16},{8,24},{16,0},{24,8},{32,48},{40,56},{48,32},{56,40},{1,17}... | collective-permute-start | bytes 1572872 | tf_op jit(solution)/shard_map/ppermute | solution.py:65
  407.7 28.2 %collective-permute-start.12 = (f32[1024,128]{0,1:T(8,128)S(1)}, f32[1024,128]{0,1:T(8,128)S(1)}, u32[]{:S(2)}, u32[]{:S(2)}) collective-permute-start(f32[1024,128]{0,1:T(8,128)S(1)} %add.105), channel_id=1, source_target_pairs={{0,32},{8,40},{16,48},{24,56},{32,0},{40,8},{48,16},{56,24},{1,33}... | collective-permute-start | bytes 1572872 | tf_op jit(solution)/shard_map/ppermute | solution.py:65
  436.0 8.0 %collective-permute-start.13 = (f32[1024,128]{0,1:T(8,128)S(1)}, f32[1024,128]{0,1:T(8,128)S(1)}, u32[]{:S(2)}, u32[]{:S(2)}) collective-permute-start(f32[1024,128]{0,1:T(8,128)S(1)} %add.106), channel_id=1, source_target_pairs={{0,4},{4,0},{1,5},{5,1},{2,6},{6,2},{3,7},{7,3},{8,12},{12,8},{9,1... | collective-permute-start | bytes 1572872 | tf_op jit(solution)/shard_map/ppermute | solution.py:65
Sparse Core Ops, SparseCore 0:
  10.8 87.1 all-gather.1
  246.5 27.4 reduce-scatter.3
  276.5 105.0 reduce-scatter.5
  384.6 25.2 reduce-scatter.7
where the time goes:
time: 452 us
  waiting for transfers between devices  335 us (74%)
  matrix products  52.3 us (12%)
  starting transfers between devices  24.4 us (5%)
  local copies, waits for them, and re-layouts  15.8 us (3%)
  between operations  14.2 us (3%)
  other arithmetic  10 us (2%)
    reduce_scatter x3, waiting for transfers between devices, body(): partial = lax.psum_scatter(partial, axis, scatter_dimension=0, tiled=True)  94.2 us
    all_gather x1, waiting for transfers between devices, body(): weight_cols = lax.all_gather(out_weight, SUB, axis=0, tiled=True)  90 us
    ppermute x6, waiting for transfers between devices, butterfly_sum(): lax.ppermute(value, axis, [(i, i ^ bit) for i in range(size)])  71.4 us
    ppermute x3, waiting for transfers between devices, scatter_ch(): lax.ppermute(block, 'ch', [(i, (i + k) % count) for i in range(count)])  44.2 us
    conv_general_dilated x3, matrix products, depthwise(): lax.conv_general_dilated(signal[None], kernel[:, None, :], (1,), 'VALID',...  31.8 us
    ppermute x3, waiting for transfers between devices, gather_ch(): lax.ppermute(part, 'ch', [(i, (i + k) % count) for i in range(count)])  24.8 us
    ppermute x6, starting transfers between devices, butterfly_sum(): lax.ppermute(value, axis, [(i, i ^ bit) for i in range(size)])  12.5 us
    ppermute x2, waiting for transfers between devices, from_behind(): lax.ppermute(value, axis, [(source, source + steps) for source in range(i...  9.48 us
  transfers between devices with their start and end apart: 18, of which 13 were waited for; matrix products, arithmetic and copies ran while one was open for 5% of the time, Pallas kernels for 0%

commit v1 on v0

--- a/solution.py
+++ b/solution.py
@@ -82,7 +82,13 @@
         query_wide = query_stream.astype(jnp.float32)
         gated = (query_wide * response).astype(jnp.bfloat16)
         gated_full = gather_ch(gated, chs)
-        weight_cols = lax.all_gather(out_weight, SUB, axis=0, tiled=True)
+        r1 = lax.all_to_all(
+            jnp.stack([out_weight for _ in range(lax.axis_size(SUB))], axis=0),
+            axis_name=SUB,
+            split_axis=0,
+            concat_axis=0,
+        )
+        weight_cols = jnp.concatenate(r1, axis=0)
         mixed = jnp.dot(gated_full, weight_cols, preferred_element_type=jnp.float32).astype(
             jnp.bfloat16
         )

time: 452 us -> 565 us (1.25)
  waiting for transfers between devices: 335 us -> 430 us
  starting transfers between devices: 24.4 us -> 36.8 us
    all_to_all x0 -> x1, waiting for transfers between devices: none -> 186 us  [body(): lax.all_to_all(jnp.stack([out_weight for _ in range(lax.axis_size(SUB))],...]
    all_gather x1 -> x0, waiting for transfers between devices: 90 us -> none  [body(): weight_cols = lax.all_gather(out_weight, SUB, axis=0, tiled=True)]
    all_to_all x0 -> x1, starting transfers between devices: none -> 13.3 us  [body(): lax.all_to_all(jnp.stack([out_weight for _ in range(lax.axis_size(SUB))],...]
  transfers between devices with their start and end apart: 18 -> 18, of which waited for: 13 -> 14; matrix products, arithmetic and copies ran while one was open for 5% -> 4% of each run, Pallas kernels for 0% -> 0%
where the time goes in v1:
time: 565 us
  waiting for transfers between devices  430 us (76%)
  matrix products  52.2 us (9%)
  starting transfers between devices  36.8 us (7%)
  local copies, waits for them, and re-layouts  21.1 us (4%)
  between operations  14.2 us (3%)
  other arithmetic  10 us (2%)
    all_to_all x1, waiting for transfers between devices, body(): lax.all_to_all(jnp.stack([out_weight for _ in range(lax.axis_size(SUB))],...  186 us
    reduce_scatter x3, waiting for transfers between devices, body(): partial = lax.psum_scatter(partial, axis, scatter_dimension=0, tiled=True)  93.6 us
    ppermute x6, waiting for transfers between devices, butterfly_sum(): lax.ppermute(value, axis, [(i, i ^ bit) for i in range(size)])  71.5 us
    ppermute x3, waiting for transfers between devices, scatter_ch(): lax.ppermute(block, 'ch', [(i, (i + k) % count) for i in range(count)])  44.9 us
    conv_general_dilated x3, matrix products, depthwise(): lax.conv_general_dilated(signal[None], kernel[:, None, :], (1,), 'VALID',...  31.8 us
    ppermute x3, waiting for transfers between devices, gather_ch(): lax.ppermute(part, 'ch', [(i, (i + k) % count) for i in range(count)])  24.5 us
    all_to_all x1, starting transfers between devices, body(): lax.all_to_all(jnp.stack([out_weight for _ in range(lax.axis_size(SUB))],...  13.3 us
    ppermute x6, starting transfers between devices, butterfly_sum(): lax.ppermute(value, axis, [(i, i ^ bit) for i in range(size)])  12.5 us
  transfers between devices with their start and end apart: 18, of which 14 were waited for; matrix products, arithmetic and copies ran while one was open for 4% of the time, Pallas kernels for 0%

profile of v1, /device:TPU:1, one launch (start us, length us, event | category | flops | bytes accessed | tf_op | source)
XLA Modules:
  0.0 564.6 jit_solution(9298236279008608697)
XLA Ops:
  7.2 5.3 stack.17
  12.5 13.3 %all-to-all-start = ((bf16[64,64,1024]{2,1,0:T(8,128)(2,1)}), bf16[64,64,1024]{2,1,0:T(8,128)(2,1)}, u32[]{:S(2)}, u32[]{:S(2)}) async-start(bf16[64,64,1024]{2,1,0:T(8,128)(2,1)} %stack.17), calls=%async_computation | async-start | bytes 16777216 | tf_op jit(solution)/shard_map/all_to_all | solution.py:85
  25.9 185.6 %all-to-all-done = bf16[64,64,1024]{2,1,0:T(8,128)(2,1)} async-done(((bf16[64,64,1024]{2,1,0:T(8,128)(2,1)}), bf16[64,64,1024]{2,1,0:T(8,128)(2,1)}, u32[]{:S(2)}, u32[]{:S(2)}) %all-to-all-start) | async-done | bytes 8388640 | tf_op jit(solution)/shard_map/all_to_all | solution.py:85
  211.6 5.7 %fusion.27 = f32[256,4096]{1,0:T(8,128)S(1)} fusion(bf16[256,1024]{1,0:T(8,128)(2,1)S(1)} %copy-done, bf16[4096,1024]{1,0:T(8,128)(2,1)} %bitcast.12), kind=kOutput, calls=%fused_computation.51 | convolution fusion | flops 2147483648 | bytes 13107200 | tf_op jit(solution)/shard_map/dot_general | solution.py:95
  217.3 1.7 constant_dynamic-slice_fusion.2
  219.1 1.2 copy-done.4
  220.2 1.2 collective-permute-start.4
  221.5 1.5 collective-permute-start.6
  222.9 1.5 collective-permute-start.5
  224.5 22.3 %collective-permute-done.4 = f32[256,1024]{1,0:T(8,128)S(1)} collective-permute-done((f32[256,1024]{1,0:T(8,128)}, f32[256,1024]{1,0:T(8,128)S(1)}, u32[]{:S(2)}, u32[]{:S(2)}) %collective-permute-start.4) | collective-permute-done | bytes 1048608 | tf_op jit(solution)/shard_map/ppermute | solution.py:57
  247.8 22.6 %collective-permute-done.5 = f32[256,1024]{1,0:T(8,128)} collective-permute-done((f32[256,1024]{1,0:T(8,128)}, f32[256,1024]{1,0:T(8,128)}, u32[]{:S(2)}, u32[]{:S(2)}) %collective-permute-start.5) | collective-permute-done | bytes 1048608 | tf_op jit(solution)/shard_map/ppermute | solution.py:57
  270.4 3.8 convert_multiply_fusion.3
  274.2 2.3 collective-permute-start.7
  277.0 7.8 %collective-permute-done.7 = f32[127,1024]{1,0:T(8,128)} collective-permute-done((f32[127,1024]{1,0:T(8,128)S(1)}, f32[127,1024]{1,0:T(8,128)}, u32[]{:S(2)}, u32[]{:S(2)}) %collective-permute-start.7) | collective-permute-done | bytes 520224 | tf_op jit(solution)/shard_map/ppermute | solution.py:25
  284.8 1.2 maximum_bitcast_fusion.1
  286.0 10.6 %fusion.8 = f32[1,256,1024]{2,0,1:T(1,128)S(1)} fusion(f32[128,1,1024]{2,1,0:T(1,128)S(1)} %copy.20, f32[1,383,1024]{2,1,0:T(8,128)S(1)} %maximum_bitcast_fusion.1), kind=kOutput, calls=%fused_computation.12 | convolution fusion | flops 402653184 | bytes 3141632 | tf_op jit(solution)/shard_map/conv_general_dilated | solution.py:29
  296.6 1.5 fusion.18
  298.2 1.9 collective-permute-start
  301.3 2.1 collective-permute-done
  303.6 10.6 %fusion.15 = f32[1,256,1024]{2,0,1:T(1,128)S(1)} fusion(f32[128,1,1024]{2,1,0:T(1,128)S(1)} %copy.18, bf16[1,383,1024]{2,1,0:T(8,128)(2,1)S(1)} %maximum_bitcast_fusion.2), kind=kOutput, calls=%fused_computation.22 | convolution fusion | flops 402653184 | bytes 2357248 | tf_op jit(solution)/shard_map/conv_general_dilated | solution.py:29
  314.2 1.2 fusion.21
  315.5 1.2 collective-permute-start.3
  316.6 1.2 collective-permute-start.2
  317.9 11.5 %collective-permute-done.3 = bf16[256,1024]{1,0:T(8,128)(2,1)S(1)} collective-permute-done((bf16[256,1024]{1,0:T(8,128)(2,1)S(1)}, bf16[256,1024]{1,0:T(8,128)(2,1)S(1)}, u32[]{:S(2)}, u32[]{:S(2)}) %collective-permute-start.3) | collective-permute-done | bytes 524320 | tf_op jit(solution)/shard_map/ppermute | solution.py:44
  329.4 2.4 collective-permute-done.2
  331.8 10.6 %collective-permute-done.1 = bf16[256,1024]{1,0:T(8,128)(2,1)S(1)} collective-permute-done((bf16[256,1024]{1,0:T(8,128)(2,1)S(1)}, bf16[256,1024]{1,0:T(8,128)(2,1)S(1)}, u32[]{:S(2)}, u32[]{:S(2)}) %collective-permute-start.1) | collective-permute-done | bytes 524320 | tf_op jit(solution)/shard_map/ppermute | solution.py:44
  342.4 1.6 pad_maximum_fusion
  344.0 2.3 gather_fusion
  346.3 2.0 fusion.26
  348.3 1.3 copy.23
  349.6 1.2 copy.25
  351.8 8.1 %fusion.28 = f32[4096,1024]{1,0:T(8,128)} fusion(bf16[256,4096]{0,1:T(8,128)(2,1)S(1)} %bitcast.51, bf16[256,1024]{1,0:T(8,128)(2,1)S(1)} %copy-done), kind=kOutput, calls=%fused_computation.52 | convolution fusion | flops 2147483648 | bytes 19398656 | tf_op jit(solution)/shard_map/dot_general | solution.py:112
  359.9 27.0 %reduce-scatter.4.cloned.1.call-done = f32[2048,1024]{1,0:T(8,128)} async-done(((f32[4096,1024]{1,0:T(8,128)}), f32[2048,1024]{1,0:T(8,128)}) %reduce-scatter.4.cloned.1.call-update) | async-done | bytes 8388624 | tf_op jit(solution)/shard_map/reduce_scatter | solution.py:116
  387.0 1.2 copy-done.2
  388.4 10.6 %fusion.13 = f32[1,128,1024]{2,0,1:T(1,128)S(1)} fusion(bf16[1,383,1024]{2,1,0:T(8,128)(2,1)S(1)} %copy-done.12, f32[256,1,1024]{2,0,1:T(8,128)S(1)} %bitcast.52), kind=kOutput, calls=%fused_computation.20 | convolution fusion | flops 402653184 | bytes 2357248 | tf_op jit(solution)/shard_map/conv_general_dilated | solution.py:29
  399.4 1.1 collective-permute-start.8
  400.4 12.3 %collective-permute-done.8 = f32[1024,128]{0,1:T(8,128)S(1)} collective-permute-done((f32[1024,128]{0,1:T(8,128)S(1)}, f32[1024,128]{0,1:T(8,128)S(1)}, u32[]{:S(2)}, u32[]{:S(2)}) %collective-permute-start.8) | collective-permute-done | bytes 524320 | tf_op jit(solution)/shard_map/ppermute | solution.py:65
  412.8 2.6 collective-permute-start.9
  415.4 11.4 %collective-permute-done.9 = f32[1024,128]{0,1:T(8,128)S(1)} collective-permute-done((f32[1024,128]{0,1:T(8,128)S(1)}, f32[1024,128]{0,1:T(8,128)S(1)}, u32[]{:S(2)}, u32[]{:S(2)}) %collective-permute-start.9) | collective-permute-done | bytes 524320 | tf_op jit(solution)/shard_map/ppermute | solution.py:65
  426.8 1.1 collective-permute-start.10
  427.9 66.6 %reduce-scatter.6.cloned.1.call-done = f32[256,1024]{1,0:T(8,128)} async-done(((f32[2048,1024]{1,0:T(8,128)}), f32[256,1024]{1,0:T(8,128)}) %reduce-scatter.6.cloned.1.call-update) | async-done | bytes 1048592 | tf_op jit(solution)/shard_map/reduce_scatter | solution.py:116
  494.7 2.4 collective-permute-start.11
  497.1 23.5 %collective-permute-done.11 = f32[1024,128]{0,1:T(8,128)S(1)} collective-permute-done((f32[1024,128]{0,1:T(8,128)S(1)}, f32[1024,128]{0,1:T(8,128)S(1)}, u32[]{:S(2)}, u32[]{:S(2)}) %collective-permute-start.11) | collective-permute-done | bytes 524320 | tf_op jit(solution)/shard_map/ppermute | solution.py:65
  520.7 4.0 collective-permute-start.12
  524.7 24.3 %collective-permute-done.12 = f32[1024,128]{0,1:T(8,128)S(1)} collective-permute-done((f32[1024,128]{0,1:T(8,128)S(1)}, f32[1024,128]{0,1:T(8,128)S(1)}, u32[]{:S(2)}, u32[]{:S(2)}) %collective-permute-start.12) | collective-permute-done | bytes 524320 | tf_op jit(solution)/shard_map/ppermute | solution.py:65
  549.0 1.4 collective-permute-start.13
  550.5 6.6 %fusion.10 = bf16[256,1024]{1,0:T(8,128)(2,1)} fusion(bf16[4096,1024]{1,0:T(8,128)(2,1)} %bitcast.12, bf16[256,1024]{1,0:T(8,128)(2,1)S(1)} %copy-done.18, bf16[256,1024]{1,0:T(8,128)(2,1)S(1)} %copy-done.17, bf16[256,1024]{1,0:T(8,128)(2,1)S(1)} %copy-done.16, bf16[256,1024]{1,0:T(8,128)(2,1)S(1)} %copy-done.15), kind=kOutput, calls=%fused_computation.19 | convolution fusion | flops 2156134400 | bytes 11010048 | tf_op jit(solution)/shard_map/dot_general | solution.py:92
  557.1 1.0 copy.28
  (67 shorter events, 4.9 us)
Async XLA Ops:
  7.2 204.4 %copy-start = (bf16[256,1024]{1,0:T(8,128)(2,1)S(1)}, bf16[256,1024]{1,0:T(8,128)(2,1)}, u32[]{:S(2)}) copy-start(bf16[256,1024]{1,0:T(8,128)(2,1)} %param.11) | copy-start | bytes 1572868
  12.5 199.1 %all-to-all-start = ((bf16[64,64,1024]{2,1,0:T(8,128)(2,1)}), bf16[64,64,1024]{2,1,0:T(8,128)(2,1)}, u32[]{:S(2)}, u32[]{:S(2)}) async-start(bf16[64,64,1024]{2,1,0:T(8,128)(2,1)} %stack.17), calls=%async_computation | async-start | bytes 16777216 | tf_op jit(solution)/shard_map/all_to_all | solution.py:85
  25.8 361.1 %reduce-scatter.4.cloned.1.call-start = ((), (), s32[]{:S(2)}) async-start(), calls=%async_computation.4 | async-start | bytes 25165824 | tf_op jit(solution)/shard_map/reduce_scatter | solution.py:116
  217.3 2.9 copy-start.4
  217.3 53.0 %copy-start.8 = (bf16[256,1024]{1,0:T(8,128)(2,1)S(1)}, bf16[256,1024]{1,0:T(8,128)(2,1)}, u32[]{:S(2)}) copy-start(bf16[256,1024]{1,0:T(8,128)(2,1)} %param.6) | copy-start | bytes 1572868
  220.2 26.6 %collective-permute-start.4 = (f32[256,1024]{1,0:T(8,128)}, f32[256,1024]{1,0:T(8,128)S(1)}, u32[]{:S(2)}, u32[]{:S(2)}) collective-permute-start(f32[256,1024]{1,0:T(8,128)} %get-tuple-element.20), channel_id=1, source_target_pairs={{0,1},{1,2},{2,3},{3,0},{4,5},{5,6},{6,7},{7,4},{8,9},{9,10},{10,1... | collective-permute-start | bytes 3145736 | tf_op jit(solution)/shard_map/ppermute | solution.py:57
  221.5 25.4 %collective-permute-start.6 = (f32[256,1024]{1,0:T(8,128)}, f32[256,1024]{1,0:T(8,128)}, u32[]{:S(2)}, u32[]{:S(2)}) collective-permute-start(f32[256,1024]{1,0:T(8,128)} %get-tuple-element.21), channel_id=1, source_target_pairs={{0,3},{1,0},{2,1},{3,2},{4,7},{5,4},{6,5},{7,6},{8,11},{9,8},{10,9... | collective-permute-start | bytes 3145736 | tf_op jit(solution)/shard_map/ppermute | solution.py:57
  222.9 47.5 %collective-permute-start.5 = (f32[256,1024]{1,0:T(8,128)}, f32[256,1024]{1,0:T(8,128)}, u32[]{:S(2)}, u32[]{:S(2)}) collective-permute-start(f32[256,1024]{1,0:T(8,128)} %get-tuple-element.22), channel_id=1, source_target_pairs={{0,2},{1,3},{2,0},{3,1},{4,6},{5,7},{6,4},{7,5},{8,10},{9,11},{10,... | collective-permute-start | bytes 3145736 | tf_op jit(solution)/shard_map/ppermute | solution.py:57
  224.5 52.1 %copy-start.6 = (f32[1024,128]{1,0:T(8,128)S(1)}, f32[1024,128]{1,0:T(8,128)}, u32[]{:S(2)}) copy-start(f32[1024,128]{1,0:T(8,128)} %param.9) | copy-start | bytes 1572868
  246.8 1.0 copy-start.10
  274.1 11.8 %copy-start.1 = (f32[256,1024]{1,0:T(8,128)}, f32[256,1024]{1,0:T(8,128)S(1)}, u32[]{:S(2)}) copy-start(f32[256,1024]{1,0:T(8,128)S(1)} %get-tuple-element.18) | copy-start | bytes 3145732
  274.2 10.6 %collective-permute-start.7 = (f32[127,1024]{1,0:T(8,128)S(1)}, f32[127,1024]{1,0:T(8,128)}, u32[]{:S(2)}, u32[]{:S(2)}) collective-permute-start(f32[127,1024]{1,0:T(8,128)S(1)} %slice.31), channel_id=1, source_target_pairs={{4,0},{8,4},{12,8},{16,12},{20,16},{24,20},{28,24},{32,28},{36,32}... | collective-permute-start | bytes 1560584 | tf_op jit(solution)/shard_map/ppermute | solution.py:25
  286.0 10.6 %copy-start.13 = (bf16[256,1024]{1,0:T(8,128)(2,1)S(1)}, bf16[256,1024]{1,0:T(8,128)(2,1)}, u32[]{:S(2)}) copy-start(bf16[256,1024]{1,0:T(8,128)(2,1)} %param.7) | copy-start | bytes 1572868
  286.0 10.6 %copy-start.14 = (bf16[256,1024]{1,0:T(8,128)(2,1)S(1)}, bf16[256,1024]{1,0:T(8,128)(2,1)}, u32[]{:S(2)}) copy-start(bf16[256,1024]{1,0:T(8,128)(2,1)} %param.8) | copy-start | bytes 1572868
  296.6 3.5 copy-start.7
  298.2 5.2 collective-permute-start
  303.5 10.7 %copy-start.11 = (bf16[1,383,1024]{2,1,0:T(8,128)(2,1)}, bf16[1,383,1024]{2,1,0:T(8,128)(2,1)S(1)}, u32[]{:S(2)}) copy-start(bf16[1,383,1024]{2,1,0:T(8,128)(2,1)S(1)} %maximum_bitcast_fusion.2) | copy-start | bytes 2353156
  303.6 10.7 %copy-start.3 = (f32[256,1024]{1,0:T(8,128)S(1)}, f32[256,1024]{1,0:T(8,128)}, u32[]{:S(2)}) copy-start(f32[256,1024]{1,0:T(8,128)} %get-tuple-element.19) | copy-start | bytes 3145732
  303.6 10.7 %copy-start.9 = (bf16[256,1024]{1,0:T(8,128)(2,1)S(1)}, bf16[256,1024]{1,0:T(8,128)(2,1)}, u32[]{:S(2)}) copy-start(bf16[256,1024]{1,0:T(8,128)(2,1)} %param.6) | copy-start | bytes 1572868
  315.5 13.9 %collective-permute-start.3 = (bf16[256,1024]{1,0:T(8,128)(2,1)S(1)}, bf16[256,1024]{1,0:T(8,128)(2,1)S(1)}, u32[]{:S(2)}, u32[]{:S(2)}) collective-permute-start(bf16[256,1024]{1,0:T(8,128)(2,1)S(1)} %get-tuple-element.35), channel_id=1, source_target_pairs={{0,3},{1,0},{2,1},{3,2},{4,7},{5,4},{6,5},{7,6},{8,11},{9,8},{10,9... | collective-permute-start | bytes 1572872 | tf_op jit(solution)/shard_map/ppermute | solution.py:44
  316.6 15.2 %collective-permute-start.2 = (bf16[256,1024]{1,0:T(8,128)(2,1)S(1)}, bf16[256,1024]{1,0:T(8,128)(2,1)S(1)}, u32[]{:S(2)}, u32[]{:S(2)}) collective-permute-start(bf16[256,1024]{1,0:T(8,128)(2,1)S(1)} %get-tuple-element.35), channel_id=1, source_target_pairs={{0,2},{1,3},{2,0},{3,1},{4,6},{5,7},{6,4},{7,5},{8,10},{9,11},{10,... | collective-permute-start | bytes 1572872 | tf_op jit(solution)/shard_map/ppermute | solution.py:44
  317.8 24.6 %collective-permute-start.1 = (bf16[256,1024]{1,0:T(8,128)(2,1)S(1)}, bf16[256,1024]{1,0:T(8,128)(2,1)S(1)}, u32[]{:S(2)}, u32[]{:S(2)}) collective-permute-start(bf16[256,1024]{1,0:T(8,128)(2,1)S(1)} %get-tuple-element.35), channel_id=1, source_target_pairs={{0,1},{1,2},{2,3},{3,0},{4,5},{5,6},{6,7},{7,4},{8,9},{9,10},{10,1... | collective-permute-start | bytes 1572872 | tf_op jit(solution)/shard_map/ppermute | solution.py:44
  348.3 2.6 copy-start.5
  359.9 134.7 %reduce-scatter.6.cloned.1.call-start = ((), (), s32[]{:S(2)}) async-start(), calls=%async_computation.5 | async-start | bytes 9437184 | tf_op jit(solution)/shard_map/reduce_scatter | solution.py:116
  386.9 1.2 copy-start.2
  386.9 1.4 copy-start.12
  387.0 171.1 %reduce-scatter.8.cloned.1.call-start = ((), (), s32[]{:S(2)}) async-start(), calls=%async_computation.6 | async-start | bytes 1310720 | tf_op jit(solution)/shard_map/reduce_scatter | solution.py:116
  399.4 13.3 %collective-permute-start.8 = (f32[1024,128]{0,1:T(8,128)S(1)}, f32[1024,128]{0,1:T(8,128)S(1)}, u32[]{:S(2)}, u32[]{:S(2)}) collective-permute-start(f32[1024,128]{0,1:T(8,128)S(1)} %bitcast.53), channel_id=1, source_target_pairs={{0,64},{64,0},{128,192},{192,128},{1,65},{65,1},{129,193},{193,129... | collective-permute-start | bytes 1572872 | tf_op jit(solution)/shard_map/ppermute | solution.py:65
  412.8 14.0 %collective-permute-start.9 = (f32[1024,128]{0,1:T(8,128)S(1)}, f32[1024,128]{0,1:T(8,128)S(1)}, u32[]{:S(2)}, u32[]{:S(2)}) collective-permute-start(f32[1024,128]{0,1:T(8,128)S(1)} %bitcast_add_fusion), channel_id=1, source_target_pairs={{0,128},{64,192},{128,0},{192,64},{1,129},{65,193},{129,1},{193,65... | collective-permute-start | bytes 1572872 | tf_op jit(solution)/shard_map/ppermute | solution.py:65
  426.8 67.8 %collective-permute-start.10 = (f32[1024,128]{0,1:T(8,128)S(1)}, f32[1024,128]{0,1:T(8,128)S(1)}, u32[]{:S(2)}, u32[]{:S(2)}) collective-permute-start(f32[1024,128]{0,1:T(8,128)S(1)} %add.103), channel_id=1, source_target_pairs={{0,8},{8,0},{16,24},{24,16},{32,40},{40,32},{48,56},{56,48},{1,9},... | collective-permute-start | bytes 1572872 | tf_op jit(solution)/shard_map/ppermute | solution.py:65
  494.6 55.8 %copy-start.15 = (bf16[256,1024]{1,0:T(8,128)(2,1)S(1)}, bf16[256,1024]{1,0:T(8,128)(2,1)}, u32[]{:S(2)}) copy-start(bf16[256,1024]{1,0:T(8,128)(2,1)} %get-tuple-element.24) | copy-start | bytes 1572868
  494.6 55.8 %copy-start.16 = (bf16[256,1024]{1,0:T(8,128)(2,1)S(1)}, bf16[256,1024]{1,0:T(8,128)(2,1)}, u32[]{:S(2)}) copy-start(bf16[256,1024]{1,0:T(8,128)(2,1)} %get-tuple-element.25) | copy-start | bytes 1572868
  494.6 55.8 %copy-start.17 = (bf16[256,1024]{1,0:T(8,128)(2,1)S(1)}, bf16[256,1024]{1,0:T(8,128)(2,1)}, u32[]{:S(2)}) copy-start(bf16[256,1024]{1,0:T(8,128)(2,1)} %get-tuple-element.26) | copy-start | bytes 1572868
  494.6 55.8 %copy-start.18 = (bf16[256,1024]{1,0:T(8,128)(2,1)S(1)}, bf16[256,1024]{1,0:T(8,128)(2,1)}, u32[]{:S(2)}) copy-start(bf16[256,1024]{1,0:T(8,128)(2,1)} %get-tuple-element.27) | copy-start | bytes 1572868
  494.7 25.9 %collective-permute-start.11 = (f32[1024,128]{0,1:T(8,128)S(1)}, f32[1024,128]{0,1:T(8,128)S(1)}, u32[]{:S(2)}, u32[]{:S(2)}) collective-permute-start(f32[1024,128]{0,1:T(8,128)S(1)} %add.104), channel_id=1, source_target_pairs={{0,16},{8,24},{16,0},{24,8},{32,48},{40,56},{48,32},{56,40},{1,17}... | collective-permute-start | bytes 1572872 | tf_op jit(solution)/shard_map/ppermute | solution.py:65
  520.7 28.3 %collective-permute-start.12 = (f32[1024,128]{0,1:T(8,128)S(1)}, f32[1024,128]{0,1:T(8,128)S(1)}, u32[]{:S(2)}, u32[]{:S(2)}) collective-permute-start(f32[1024,128]{0,1:T(8,128)S(1)} %add.105), channel_id=1, source_target_pairs={{0,32},{8,40},{16,48},{24,56},{32,0},{40,8},{48,16},{56,24},{1,33}... | collective-permute-start | bytes 1572872 | tf_op jit(solution)/shard_map/ppermute | solution.py:65
  549.0 8.0 %collective-permute-start.13 = (f32[1024,128]{0,1:T(8,128)S(1)}, f32[1024,128]{0,1:T(8,128)S(1)}, u32[]{:S(2)}, u32[]{:S(2)}) collective-permute-start(f32[1024,128]{0,1:T(8,128)S(1)} %add.106), channel_id=1, source_target_pairs={{0,4},{4,0},{1,5},{5,1},{2,6},{6,2},{3,7},{7,3},{8,12},{12,8},{9,1... | collective-permute-start | bytes 1572872 | tf_op jit(solution)/shard_map/ppermute | solution.py:65
Sparse Core Ops, SparseCore 0:
  360.0 26.8 reduce-scatter.3
  389.5 105.0 reduce-scatter.5
  497.7 25.3 reduce-scatter.7
